TPU v7x, 32 devices: a whole 2x2x4 slice. The times are simulated.
32 devices in a mesh: tok: 8 (over z, core), head: 4 (over y, x).
Axes of the slice: x: 2, y: 2, z: 4, core: 2. Of those that a mesh axis runs over, the one named last changes fastest.
Arguments:
- query_states: bfloat16 [12288, 3072], P('tok', 'head')
- key_states: bfloat16 [12288, 3072], P('tok', 'head')
- value_states: bfloat16 [12288, 3072], P('tok', 'head'), may hold values from -6 to 6
- query_gain: float32 [3072], P('head'), may hold values from 1 to 2.5
- key_gain: float32 [3072], P('head'), may hold values from 1 to 2.5
- windows: int32 [48, 27], P('tok'), may hold values from -1 to 47, as said below
Outputs:
- attention: bfloat16 [12288, 3072], P('tok', 'head')
Inputs may be any that keep to these rules, and one draw needn't show every extreme that they name: Slots 0 to 8 of windows[i] name tiles of the tile-frame before tile i's, the next 9 tiles of its own tile-frame, the last 9 tiles of the tile-frame after it; in each group the named tiles come first and -1 fills the rest; tile i itself is always named; no tile is named twice in a row; a named tile's tile row and tile column differ from tile i's by at most 2 each, and some named tiles differ by 2 in both.
All inputs are finite; a program needn't handle non-finite values.
Results may differ from a plain program's by a relative error of at most 0.012.
The roundings to bfloat16 on the way count: a program that leaves them out, or rounds other values in their place, can miss the bound.
Values may be sent and summed in bfloat16 or wider, within the bound.
No kernel may reach another device: no remote copies, remote signals or barrier semaphores. Data moves between devices by JAX's collectives and lax.ppermute only.
A program may use at most 320 MiB of HBM per device.

v0:
```python
import math
import jax
import jax.numpy as jnp
from jax import lax
from jax.sharding import PartitionSpec as P

HEAD_DIM = 128
MODEL_DIM = 3072
TILE_TOKENS = 256
WINDOW_SLOTS = 27


def square_sums(source):
    widened = source.astype(jnp.float32)
    return jnp.sum(widened * widened, axis=1)


def normalize_rows(source, totals, scale_gain):
    widened = source.astype(jnp.float32)
    return (widened * lax.rsqrt(totals[:, None] / MODEL_DIM + 1e-06) * scale_gain).astype(
        jnp.bfloat16
    )


def on_device(query_states, key_states, value_states, query_gain, key_gain, windows):
    row_count = query_states.shape[0]
    local_width = query_states.shape[1]
    local_tiles = windows.shape[0]
    query_total, key_total = lax.psum((square_sums(query_states), square_sums(key_states)), "head")
    query_normed = normalize_rows(query_states, query_total, query_gain)
    sent_keys = normalize_rows(key_states, key_total, key_gain)
    paired = jnp.stack([sent_keys, value_states])
    extended = lax.all_gather(paired, "tok", axis=1, tiled=True)
    key_window_rows = extended[0]
    heads_here = local_width // HEAD_DIM
    key_tiles = key_window_rows.reshape(-1, TILE_TOKENS, local_width)
    value_tiles = extended[1].reshape(-1, TILE_TOKENS, local_width)
    query_tiles = query_normed.reshape(local_tiles, TILE_TOKENS, local_width)
    valid_slots = windows >= 0
    local_ids = jnp.where(valid_slots, windows, 0)
    block_count = local_tiles // 2
    score_scale = 1.0 / math.sqrt(HEAD_DIM)

    def attend(block_index):
        block_start = block_index * 2
        query_block = lax.dynamic_slice_in_dim(query_tiles, block_start, 2, 0)
        tile_ids = lax.dynamic_slice_in_dim(local_ids, block_start, 2, 0)
        live_slots = lax.dynamic_slice_in_dim(valid_slots, block_start, 2, 0)
        key_window = key_tiles[tile_ids].reshape(2, WINDOW_SLOTS * TILE_TOKENS, local_width)
        value_window = value_tiles[tile_ids].reshape(2, WINDOW_SLOTS * TILE_TOKENS, local_width)
        key_mask = jnp.repeat(live_slots, TILE_TOKENS, axis=1)[:, None, :]
        results = []
        for head_number in range(heads_here):
            lower = head_number * HEAD_DIM
            upper = lower + HEAD_DIM
            scores = (
                jnp.einsum(
                    "tqd,tkd->tqk",
                    query_block[:, :, lower:upper],
                    key_window[:, :, lower:upper],
                    preferred_element_type=jnp.float32,
                )
                * score_scale
            )
            scores = jnp.where(key_mask, scores, -jnp.inf)
            row_max = jnp.max(scores, axis=2, keepdims=True)
            weights = jnp.exp(scores - row_max)
            weight_sum = jnp.sum(weights, axis=2, keepdims=True)
            mixed = jnp.einsum(
                "tqk,tkd->tqd",
                weights.astype(jnp.bfloat16),
                value_window[:, :, lower:upper],
                preferred_element_type=jnp.float32,
            )
            results.append((mixed / weight_sum).astype(jnp.bfloat16))
        return jnp.concatenate(results, axis=2)

    outputs = lax.map(attend, jnp.arange(block_count, dtype=jnp.int32))
    return outputs.reshape(row_count, local_width)


def solution(mesh):
    in_specs = (
        P("tok", "head"),
        P("tok", "head"),
        P("tok", "head"),
        P("head"),
        P("head"),
        P("tok", None),
    )
    out_specs = P("tok", "head")
    return jax.shard_map(
        on_device, mesh=mesh, in_specs=in_specs, out_specs=out_specs, check_vma=False
    )
```

profile of v0, /device:TPU:0, one launch (start us, length us, event | category | flops | bytes accessed | tf_op | source)
XLA Modules:
  0.0 967.4 jit_solution(3506104877108742249)
XLA Ops:
  6.5 2.4 fusion.168
  8.9 2.2 fusion.171
  11.1 17.5 %all-reduce = (f32[1536]{0:T(1024)S(1)}, f32[1536]{0:T(1024)S(1)}) all-reduce(f32[1536]{0:T(1024)S(1)} %fusion.168, f32[1536]{0:T(1024)S(1)} %fusion.171), channel_id=1, replica_groups=mesh['tok'=8,'head'=4] {'head'}, use_global_device_ids=true, to_apply=%region_1.0 | all-reduce | flops 3072 | bytes 24576 | tf_op jit(solution)/shard_map/psum | solution.py:29
  28.6 2.3 fusion.174
  30.9 4.3 pad_maximum_fusion
  35.3 2.0 fusion.170
  37.3 320.6 %all-gather.2.cloned.1.call-done = bf16[2,12288,768]{2,1,0:T(8,128)(2,1)} async-done(((bf16[2,1536,768]{2,1,0:T(8,128)(2,1)}), bf16[2,12288,768]{2,1,0:T(8,128)(2,1)}) %all-gather.2.cloned.1.call-update) | async-done | bytes 37748752 | tf_op jit(solution)/shard_map/all_gather | solution.py:33
  357.9 26.5 %fusion.175 = (bf16[1,12288,768]{2,1,0:T(8,128)(2,1)}, bf16[1,12288,768]{2,1,0:T(8,128)(2,1)}) fusion(bf16[2,12288,768]{2,1,0:T(8,128)(2,1)} %all-gather.2.cloned.1.call-done), kind=kLoop, calls=%fused_computation.126 | loop fusion | bytes 75497472 | tf_op jit(solution)/shard_map/slice | solution.py:37
  384.4 575.9 %while.10 = (s32[]{:T(128)}, bf16[3,2,256,768]{3,2,1,0:T(8,128)(2,1)}, s32[3]{0:T(128)S(1)}, pred[6,27]{1,0:T(8,128)(4,1)S(1)}, bf16[6,256,768]{2,1,0:T(8,128)(2...) while((s32[]{:T(128)}, ...), condition=%wide.region_17.18_spmd, body=%wide.region_4.17_spmd.sunk | while | flops 11105987584 | bytes 443850720 | solution.py:78
  384.6 0.7 dynamic_slice.22
  386.0 0.1 reshape.71
  386.1 15.5 %gather_fusion.1 = bf16[54,256,768]{2,1,0:T(8,128)(2,1)} fusion(bf16[48,256,768]{2,1,0:T(8,128)(2,1)} %get-tuple-element.201, s32[1024]{0:T(1024)S(1)} %pad_clamp_fusion.2), kind=kCustom, calls=%fused_computation.clone.1 | custom fusion | bytes 42467544 | tf_op jit(solution)/shard_map/while/body/eval_jaxpr/gather | solution.py:49
  401.6 9.1 fusion.229
  410.8 10.7 %fusion.230 = (f32[2,256]{1,0:T(2,128)S(1)}, f32[2,256]{1,0:T(2,128)S(1)}, f32[2,256,6912]{2,1,0:T(8,128)}) fusion(pred[2,6912]{1,0:T(4,128)(4,1)S(1)} %bitcast.41, f32[2,256,6912]{2,1,0:T(8,128)} %fusion.229, bf16[2,6912,768]{2,1,0:T(8,128)(2,1)} %bitcast.27, bf16[6,256,768]{2,1,0:T(8,128)(2,1)} %get-tuple-element.199, s32[]{:T(128)S(6)} %select_n.152, ...), kind=kOutput, calls=%fused_computation.19.clone.1 | convolution fusion | flops 927202304 | bytes 31999496 | tf_op jit(solution)/shard_map/while/body/eval_jaxpr/tqd,tkd->tqk/dot_general | solution.py:57
  421.5 9.2 fusion.231
  430.7 9.0 fusion.232
  439.7 9.1 fusion.233
  448.9 31.3 %fusion.234 = (f32[2,256]{1,0:T(2,128)S(1)}, f32[2,256]{1,0:T(2,128)S(1)}, f32[2,256]{1,0:T(2,128)S(1)}, f32[2,256]{1,0:T(2,128)S(1)}, f32[2,256]{1,0:T(2,128)S(...) fusion(f32[2,256,6912]{2,1,0:T(8,128)} %get-tuple-element.148, f32[2,256]{1,0:T(2,128)S(1)} %get-tuple-element.149, ...), kind=kOutput, calls=%fused_computation.30.clone.1 | convolution fusion | flops 976745472 | bytes 88634888 | tf_op jit(solution)/shard_map/while/body/eval_jaxpr/tqd,tkd->tqk/dot_general | solution.py:57
  480.1 21.1 %fusion.236 = (f32[2,256]{1,0:T(2,128)S(1)}, f32[2,256]{1,0:T(2,128)S(1)}, f32[2,256]{1,0:T(2,128)S(1)}, f32[2,256]{1,0:T(2,128)S(1)}) fusion(f32[2,256,6912]{2,1,0:T(8,128)} %fusion.233, f32[2,256]{1,0:T(2,128)S(1)} %get-tuple-element.153, pred[2,6912]{1,0:T(4,128)(4,1)S(1)} %bitcast.43, f32[2,256]{1,0:T(2,128)S(1)} %get-tuple-element.152, ...), kind=kLoop, calls=%fused_computation.28.clone.1 | loop fusion | flops 56621056 | bytes 56653312 | tf_op jit(solution)/shard_map/while/body/eval_jaxpr/reduce_sum | solution.py:68
  501.2 16.1 %gather_fusion = bf16[54,256,768]{2,1,0:T(8,128)(2,1)} fusion(bf16[48,256,768]{2,1,0:T(8,128)(2,1)} %get-tuple-element.202, s32[1024]{0:T(1024)S(1)} %pad_clamp_fusion.2), kind=kCustom, calls=%fused_computation.1.clone.1 | custom fusion | bytes 42467544 | tf_op jit(solution)/shard_map/while/body/eval_jaxpr/gather | solution.py:50
  517.3 9.5 fusion.235
  526.8 9.5 fusion.237
  536.4 9.6 fusion.238
  545.9 9.7 %fusion.239 = bf16[2,256,768]{1,2,0:T(8,128)(2,1)S(1)} fusion(bf16[2,256,768]{1,2,0:T(8,128)(2,1)S(1)} %fusion.238, bf16[2,6912,768]{2,1,0:T(8,128)(2,1)} %bitcast.37, f32[2,256,6912]{2,1,0:T(8,128)} %fusion.232, f32[2,256]{1,0:T(2,128)S(1)} %get-tuple-element.155, pred[2,6912]{1,0:T(4,128)(4,1)S(1)} %bitcast.47, f32[2,256]{1,0:T(2,128)S(1)} %get-tuple-element.158), kind=kOutput, calls=%fused_computation.73.clone.1 | convolution fusion | flops 920256512 | bytes 17857536 | tf_op jit(solution)/shard_map/while/body/eval_jaxpr/tqk,tkd->tqd/dot_general | solution.py:69
  555.7 9.6 fusion.240
  565.2 9.6 fusion.241
  574.8 0.3 copy.27
  575.1 0.9 constant_dynamic-update-slice_fusion.2
  576.2 0.7 dynamic_slice.22
  577.7 15.6 %gather_fusion.1 = bf16[54,256,768]{2,1,0:T(8,128)(2,1)} fusion(bf16[48,256,768]{2,1,0:T(8,128)(2,1)} %get-tuple-element.201, s32[1024]{0:T(1024)S(1)} %pad_clamp_fusion.2), kind=kCustom, calls=%fused_computation.clone.1 | custom fusion | bytes 42467544 | tf_op jit(solution)/shard_map/while/body/eval_jaxpr/gather | solution.py:49
  593.3 9.1 fusion.229
  602.5 10.7 %fusion.230 = (f32[2,256]{1,0:T(2,128)S(1)}, f32[2,256]{1,0:T(2,128)S(1)}, f32[2,256,6912]{2,1,0:T(8,128)}) fusion(pred[2,6912]{1,0:T(4,128)(4,1)S(1)} %bitcast.41, f32[2,256,6912]{2,1,0:T(8,128)} %fusion.229, bf16[2,6912,768]{2,1,0:T(8,128)(2,1)} %bitcast.27, bf16[6,256,768]{2,1,0:T(8,128)(2,1)} %get-tuple-element.199, s32[]{:T(128)S(6)} %select_n.152, ...), kind=kOutput, calls=%fused_computation.19.clone.1 | convolution fusion | flops 927202304 | bytes 31999496 | tf_op jit(solution)/shard_map/while/body/eval_jaxpr/tqd,tkd->tqk/dot_general | solution.py:57
  613.2 9.2 fusion.231
  622.4 9.0 fusion.232
  631.4 9.1 fusion.233
  640.6 31.3 %fusion.234 = (f32[2,256]{1,0:T(2,128)S(1)}, f32[2,256]{1,0:T(2,128)S(1)}, f32[2,256]{1,0:T(2,128)S(1)}, f32[2,256]{1,0:T(2,128)S(1)}, f32[2,256]{1,0:T(2,128)S(...) fusion(f32[2,256,6912]{2,1,0:T(8,128)} %get-tuple-element.148, f32[2,256]{1,0:T(2,128)S(1)} %get-tuple-element.149, ...), kind=kOutput, calls=%fused_computation.30.clone.1 | convolution fusion | flops 976745472 | bytes 88634888 | tf_op jit(solution)/shard_map/while/body/eval_jaxpr/tqd,tkd->tqk/dot_general | solution.py:57
  671.9 21.1 %fusion.236 = (f32[2,256]{1,0:T(2,128)S(1)}, f32[2,256]{1,0:T(2,128)S(1)}, f32[2,256]{1,0:T(2,128)S(1)}, f32[2,256]{1,0:T(2,128)S(1)}) fusion(f32[2,256,6912]{2,1,0:T(8,128)} %fusion.233, f32[2,256]{1,0:T(2,128)S(1)} %get-tuple-element.153, pred[2,6912]{1,0:T(4,128)(4,1)S(1)} %bitcast.43, f32[2,256]{1,0:T(2,128)S(1)} %get-tuple-element.152, ...), kind=kLoop, calls=%fused_computation.28.clone.1 | loop fusion | flops 56621056 | bytes 56653312 | tf_op jit(solution)/shard_map/while/body/eval_jaxpr/reduce_sum | solution.py:68
  693.0 15.8 %gather_fusion = bf16[54,256,768]{2,1,0:T(8,128)(2,1)} fusion(bf16[48,256,768]{2,1,0:T(8,128)(2,1)} %get-tuple-element.202, s32[1024]{0:T(1024)S(1)} %pad_clamp_fusion.2), kind=kCustom, calls=%fused_computation.1.clone.1 | custom fusion | bytes 42467544 | tf_op jit(solution)/shard_map/while/body/eval_jaxpr/gather | solution.py:50
  708.8 9.6 fusion.235
  718.3 9.6 fusion.237
  727.9 9.6 fusion.238
  737.4 9.8 %fusion.239 = bf16[2,256,768]{1,2,0:T(8,128)(2,1)S(1)} fusion(bf16[2,256,768]{1,2,0:T(8,128)(2,1)S(1)} %fusion.238, bf16[2,6912,768]{2,1,0:T(8,128)(2,1)} %bitcast.37, f32[2,256,6912]{2,1,0:T(8,128)} %fusion.232, f32[2,256]{1,0:T(2,128)S(1)} %get-tuple-element.155, pred[2,6912]{1,0:T(4,128)(4,1)S(1)} %bitcast.47, f32[2,256]{1,0:T(2,128)S(1)} %get-tuple-element.158), kind=kOutput, calls=%fused_computation.73.clone.1 | convolution fusion | flops 920256512 | bytes 17857536 | tf_op jit(solution)/shard_map/while/body/eval_jaxpr/tqk,tkd->tqd/dot_general | solution.py:69
  747.2 9.6 fusion.240
  756.8 9.6 fusion.241
  766.3 0.3 copy.27
  766.6 0.9 constant_dynamic-update-slice_fusion.2
  767.9 0.7 dynamic_slice.22
  769.4 15.6 %gather_fusion.1 = bf16[54,256,768]{2,1,0:T(8,128)(2,1)} fusion(bf16[48,256,768]{2,1,0:T(8,128)(2,1)} %get-tuple-element.201, s32[1024]{0:T(1024)S(1)} %pad_clamp_fusion.2), kind=kCustom, calls=%fused_computation.clone.1 | custom fusion | bytes 42467544 | tf_op jit(solution)/shard_map/while/body/eval_jaxpr/gather | solution.py:49
  785.0 9.0 fusion.229
  794.2 10.7 %fusion.230 = (f32[2,256]{1,0:T(2,128)S(1)}, f32[2,256]{1,0:T(2,128)S(1)}, f32[2,256,6912]{2,1,0:T(8,128)}) fusion(pred[2,6912]{1,0:T(4,128)(4,1)S(1)} %bitcast.41, f32[2,256,6912]{2,1,0:T(8,128)} %fusion.229, bf16[2,6912,768]{2,1,0:T(8,128)(2,1)} %bitcast.27, bf16[6,256,768]{2,1,0:T(8,128)(2,1)} %get-tuple-element.199, s32[]{:T(128)S(6)} %select_n.152, ...), kind=kOutput, calls=%fused_computation.19.clone.1 | convolution fusion | flops 927202304 | bytes 31999496 | tf_op jit(solution)/shard_map/while/body/eval_jaxpr/tqd,tkd->tqk/dot_general | solution.py:57
  804.9 9.2 fusion.231
  814.1 9.0 fusion.232
  823.2 9.1 fusion.233
  832.3 31.1 %fusion.234 = (f32[2,256]{1,0:T(2,128)S(1)}, f32[2,256]{1,0:T(2,128)S(1)}, f32[2,256]{1,0:T(2,128)S(1)}, f32[2,256]{1,0:T(2,128)S(1)}, f32[2,256]{1,0:T(2,128)S(...) fusion(f32[2,256,6912]{2,1,0:T(8,128)} %get-tuple-element.148, f32[2,256]{1,0:T(2,128)S(1)} %get-tuple-element.149, ...), kind=kOutput, calls=%fused_computation.30.clone.1 | convolution fusion | flops 976745472 | bytes 88634888 | tf_op jit(solution)/shard_map/while/body/eval_jaxpr/tqd,tkd->tqk/dot_general | solution.py:57
  863.4 21.1 %fusion.236 = (f32[2,256]{1,0:T(2,128)S(1)}, f32[2,256]{1,0:T(2,128)S(1)}, f32[2,256]{1,0:T(2,128)S(1)}, f32[2,256]{1,0:T(2,128)S(1)}) fusion(f32[2,256,6912]{2,1,0:T(8,128)} %fusion.233, f32[2,256]{1,0:T(2,128)S(1)} %get-tuple-element.153, pred[2,6912]{1,0:T(4,128)(4,1)S(1)} %bitcast.43, f32[2,256]{1,0:T(2,128)S(1)} %get-tuple-element.152, ...), kind=kLoop, calls=%fused_computation.28.clone.1 | loop fusion | flops 56621056 | bytes 56653312 | tf_op jit(solution)/shard_map/while/body/eval_jaxpr/reduce_sum | solution.py:68
  884.5 15.8 %gather_fusion = bf16[54,256,768]{2,1,0:T(8,128)(2,1)} fusion(bf16[48,256,768]{2,1,0:T(8,128)(2,1)} %get-tuple-element.202, s32[1024]{0:T(1024)S(1)} %pad_clamp_fusion.2), kind=kCustom, calls=%fused_computation.1.clone.1 | custom fusion | bytes 42467544 | tf_op jit(solution)/shard_map/while/body/eval_jaxpr/gather | solution.py:50
  900.3 9.5 fusion.235
  909.9 9.5 fusion.237
  919.4 9.6 fusion.238
  929.0 9.9 %fusion.239 = bf16[2,256,768]{1,2,0:T(8,128)(2,1)S(1)} fusion(bf16[2,256,768]{1,2,0:T(8,128)(2,1)S(1)} %fusion.238, bf16[2,6912,768]{2,1,0:T(8,128)(2,1)} %bitcast.37, f32[2,256,6912]{2,1,0:T(8,128)} %fusion.232, f32[2,256]{1,0:T(2,128)S(1)} %get-tuple-element.155, pred[2,6912]{1,0:T(4,128)(4,1)S(1)} %bitcast.47, f32[2,256]{1,0:T(2,128)S(1)} %get-tuple-element.158), kind=kOutput, calls=%fused_computation.73.clone.1 | convolution fusion | flops 920256512 | bytes 17857536 | tf_op jit(solution)/shard_map/while/body/eval_jaxpr/tqk,tkd->tqd/dot_general | solution.py:69
  938.9 9.6 fusion.240
  948.5 9.6 fusion.241
  958.1 0.3 copy.27
  958.3 0.9 constant_dynamic-update-slice_fusion.2
  (30 shorter events, 0.6 us)
Async XLA Ops:
  6.5 28.7 %copy-start = (bf16[1536,768]{1,0:T(8,128)(2,1)S(1)}, bf16[1536,768]{1,0:T(8,128)(2,1)}, u32[]{:S(2)}) copy-start(bf16[1536,768]{1,0:T(8,128)(2,1)} %param.8) | copy-start | bytes 7077892
  6.5 28.7 %copy-start.1 = (s32[6,27]{1,0:T(8,128)S(1)}, s32[6,27]{1,0:T(8,128)}, u32[]{:S(2)}) copy-start(s32[6,27]{1,0:T(8,128)} %param.13) | copy-start | bytes 1948
  6.5 28.7 %copy-start.2 = (f32[768]{0:T(1024)S(1)}, f32[768]{0:T(1024)}, u32[]{:S(2)}) copy-start(f32[768]{0:T(1024)} %param.11) | copy-start | bytes 9220
  6.5 351.4 %all-gather.2.cloned.1.call-start = ((), (), s32[]{:S(2)}) async-start(), calls=%async_computation | async-start | bytes 42467328 | tf_op jit(solution)/shard_map/all_gather | solution.py:33
Sparse Core Ops, SparseCore 0:
  35.3 322.5 all-gather.1
where the time goes:
time: 971 us; the launch traced here: 967 us
  matrix products  408 us (42%)
  waiting for transfers between devices  321 us (33%)
  local copies, waits for them, and re-layouts  127 us (13%)
  other arithmetic  76.5 us (8%)
  blocking collectives  17.5 us (2%)
  between operations  13.7 us (1%)
    all_gather x1, waiting for transfers between devices, on_device(): extended = lax.all_gather(paired, 'tok', axis=1, tiled=True)  321 us
    dot_general x18, matrix products, attend(): jnp.einsum('tqd,tkd->tqk', query_block[:, :, lower:upper], key_window[:,...  235 us
    dot_general x18, matrix products, attend(): jnp.einsum('tqk,tkd->tqd', weights.astype(jnp.bfloat16), value_window[:,...  173 us
    reduce_sum x3, other arithmetic, attend(): weight_sum = jnp.sum(weights, axis=2, keepdims=True)  63.2 us
    gather x3, local copies, waits for them, and re-layouts, attend(): value_tiles[tile_ids].reshape(2, WINDOW_SLOTS * TILE_TOKENS, local_width)  47.6 us
    gather x3, local copies, waits for them, and re-layouts, attend(): key_tiles[tile_ids].reshape(2, WINDOW_SLOTS * TILE_TOKENS, local_width)  46.7 us
    slice x1, local copies, waits for them, and re-layouts, on_device(): value_tiles = extended[1].reshape(-1, TILE_TOKENS, local_width)  26.5 us
  transfers between devices with their start and end apart: 1, of which 1 were waited for; matrix products, arithmetic and copies ran while one was open for 0% of the time, Pallas kernels for 0%

commit v1 on v0

--- a/solution.py
+++ b/solution.py
@@ -8,6 +8,28 @@
 MODEL_DIM = 3072
 TILE_TOKENS = 256
 WINDOW_SLOTS = 27
+
+
+def in_order(blocks, dim):
+    lengths = list(blocks.shape[1:])
+    lengths[dim] *= blocks.shape[0]
+    return jnp.moveaxis(blocks, 0, dim).reshape(lengths)
+
+
+def ring_gather(x, axis, dim):
+    size = lax.axis_size(axis)
+    pairs = [(i, (i + 1) % size) for i in range(size)]
+    back = [(b, a) for a, b in pairs]
+    lower, upper = ([], [])
+    for step in range(size - 1):
+        if step % 2 == 0:
+            lower.append(lax.ppermute(lower[-1] if lower else x, axis, pairs))
+        else:
+            upper.append(lax.ppermute(upper[-1] if upper else x, axis, back))
+    blocks = jnp.stack([*lower[::-1], x, *upper])
+    shift = lax.axis_index(axis) - len(lower)
+    blocks = blocks[(jnp.arange(size) - shift) % size]
+    return in_order(blocks, dim)
 
 
 def square_sums(source):
@@ -30,7 +52,7 @@
     query_normed = normalize_rows(query_states, query_total, query_gain)
     sent_keys = normalize_rows(key_states, key_total, key_gain)
     paired = jnp.stack([sent_keys, value_states])
-    extended = lax.all_gather(paired, "tok", axis=1, tiled=True)
+    extended = ring_gather(paired, "tok", 1)
     key_window_rows = extended[0]
     heads_here = local_width // HEAD_DIM
     key_tiles = key_window_rows.reshape(-1, TILE_TOKENS, local_width)

time: 971 us -> 1130 us (1.16)
  local copies, waits for them, and re-layouts: 127 us -> 216 us
  waiting for transfers between devices: 321 us -> 357 us
  other arithmetic: 76.5 us -> 104 us
  between operations: 13.7 us -> 1.2 us
    ppermute x0 -> x7, waiting for transfers between devices: none -> 357 us  [the longest x4 357 us: ring_gather(): lower.append(lax.ppermute(lower[-1] if lower else x, axis, pairs))]
    all_gather x1 -> x0, waiting for transfers between devices: 321 us -> none  [on_device(): extended = lax.all_gather(paired, 'tok', axis=1, tiled=True)]
    gather x0 -> x4, local copies, waits for them, and re-layouts: none -> 58.4 us  [ring_gather(): blocks = blocks[(jnp.arange(size) - shift) % size]]
    unnamed x6 -> x24, local copies, waits for them, and re-layouts: 0.01 us -> 28.6 us
    transpose x0 -> x1, other arithmetic: none -> 25.9 us  [in_order(): return jnp.moveaxis(blocks, 0, dim).reshape(lengths)]
  transfers between devices with their start and end apart: 1 -> 7, of which waited for: 1 -> 4; matrix products, arithmetic and copies ran while one was open for 0% -> 3% of each run, Pallas kernels for 0% -> 0%
where the time goes in v1:
time: 1130 us; the launch traced here: 1120 us
  matrix products  408 us (36%)
  waiting for transfers between devices  357 us (32%)
  local copies, waits for them, and re-layouts  216 us (19%)
  other arithmetic  104 us (9%)
  blocking collectives  17.5 us (2%)
    ppermute x4, waiting for transfers between devices, ring_gather(): lower.append(lax.ppermute(lower[-1] if lower else x, axis, pairs))  357 us
    dot_general x18, matrix products, attend(): jnp.einsum('tqd,tkd->tqk', query_block[:, :, lower:upper], key_window[:,...  235 us
    dot_general x18, matrix products, attend(): jnp.einsum('tqk,tkd->tqd', weights.astype(jnp.bfloat16), value_window[:,...  173 us
    reduce_sum x3, other arithmetic, attend(): weight_sum = jnp.sum(weights, axis=2, keepdims=True)  63.2 us
    gather x4, local copies, waits for them, and re-layouts, ring_gather(): blocks = blocks[(jnp.arange(size) - shift) % size]  58.4 us
    gather x3, local copies, waits for them, and re-layouts, attend(): value_tiles[tile_ids].reshape(2, WINDOW_SLOTS * TILE_TOKENS, local_width)  47.5 us
    gather x3, local copies, waits for them, and re-layouts, attend(): key_tiles[tile_ids].reshape(2, WINDOW_SLOTS * TILE_TOKENS, local_width)  46.7 us
    unnamed x24, local copies, waits for them, and re-layouts  28.6 us
  transfers between devices with their start and end apart: 7, of which 4 were waited for; matrix products, arithmetic and copies ran while one was open for 3% of the time, Pallas kernels for 0%

profile of v1, /device:TPU:0, one launch (start us, length us, event | category | flops | bytes accessed | tf_op | source)
XLA Modules:
  0.0 1118.8 jit_solution(6799116763743841667)
XLA Ops:
  4.4 17.5 %all-reduce = (f32[1536]{0:T(1024)S(1)}, f32[1536]{0:T(1024)S(1)}) all-reduce(f32[1536]{0:T(1024)S(1)} %fusion.168, f32[1536]{0:T(1024)S(1)} %fusion.171), channel_id=1, replica_groups=mesh['tok'=8,'head'=4] {'head'}, use_global_device_ids=true, to_apply=%region_1.0 | all-reduce | flops 3072 | bytes 24576 | tf_op jit(solution)/shard_map/psum | solution.py:51
  26.4 55.3 %collective-permute-done = bf16[2,1536,768]{2,1,0:T(8,128)(2,1)S(1)} collective-permute-done((bf16[2,1536,768]{2,1,0:T(8,128)(2,1)S(1)}, bf16[2,1536,768]{2,1,0:T(8,128)(2,1)S(1)}, u32[]{:S(2)}, u32[]{:S(2)}) %collective-permute-start) | collective-permute-done | bytes 4718624 | tf_op jit(solution)/shard_map/ppermute | solution.py:26
  87.4 102.1 %collective-permute-done.1 = bf16[2,1536,768]{2,1,0:T(8,128)(2,1)S(1)} collective-permute-done((bf16[2,1536,768]{2,1,0:T(8,128)(2,1)S(1)}, bf16[2,1536,768]{2,1,0:T(8,128)(2,1)S(1)}, u32[]{:S(2)}, u32[]{:S(2)}) %collective-permute-start.1) | collective-permute-done | bytes 4718624 | tf_op jit(solution)/shard_map/ppermute | solution.py:26
  191.6 3.5 collective-permute-start.5
  195.2 101.5 %collective-permute-done.2 = bf16[2,1536,768]{2,1,0:T(8,128)(2,1)} collective-permute-done((bf16[2,1536,768]{2,1,0:T(8,128)(2,1)S(1)}, bf16[2,1536,768]{2,1,0:T(8,128)(2,1)}, u32[]{:S(2)}, u32[]{:S(2)}) %collective-permute-start.2) | collective-permute-done | bytes 4718624 | tf_op jit(solution)/shard_map/ppermute | solution.py:26
  296.8 3.8 fusion.170
  300.6 3.6 collective-permute-start.6
  304.2 98.5 %collective-permute-done.3 = bf16[2,1536,768]{2,1,0:T(8,128)(2,1)} collective-permute-done((bf16[2,1536,768]{2,1,0:T(8,128)(2,1)}, bf16[2,1536,768]{2,1,0:T(8,128)(2,1)}, u32[]{:S(2)}, u32[]{:S(2)}) %collective-permute-start.3) | collective-permute-done | bytes 4718624 | tf_op jit(solution)/shard_map/ppermute | solution.py:26
  402.7 4.8 bitcast_dynamic-update-slice_fusion.7
  407.5 5.0 bitcast_dynamic-update-slice_fusion.6
  419.9 4.9 bitcast_dynamic-update-slice_fusion.2
  424.8 4.7 bitcast_dynamic-update-slice_fusion.1
  432.0 25.4 %fusion.178 = (bf16[8,2,512,768]{3,2,1,0:T(8,128)(2,1)}, bf16[8,2,512,768]{3,2,1,0:T(8,128)(2,1)}, bf16[8,2,512,768]{3,2,1,0:T(8,128)(2,1)}) fusion(bf16[8,2,1536,768]{3,2,1,0:T(8,128)(2,1)} %bitcast_dynamic-update-slice_fusion), kind=kLoop, calls=%fused_computation.146 | loop fusion | bytes 75497472 | tf_op jit(solution)/shard_map/gather | solution.py:31
  457.4 11.0 gather_fusion.2
  468.4 11.0 gather_fusion.3
  479.5 10.9 gather_fusion.4
  490.4 25.9 %maximum_bitcast_fusion = bf16[2,8,1536,768]{3,2,0,1:T(8,128)(2,1)} fusion(bf16[8,2,512,768]{3,2,1,0:T(8,128)(2,1)} %gather_fusion.4, bf16[8,2,512,768]{3,2,1,0:T(8,128)(2,1)} %gather_fusion.3, bf16[8,2,512,768]{3,2,1,0:T(8,128)(2,1)} %gather_fusion.2), kind=kLoop, calls=%fused_computation.113 | loop fusion | flops 113246208 | bytes 75497472 | tf_op jit(solution)/shard_map/transpose | solution.py:16
  516.4 25.8 %fusion.177 = (bf16[1,8,1536,768]{3,2,0,1:T(8,128)(2,1)}, bf16[1,8,1536,768]{3,2,0,1:T(8,128)(2,1)}) fusion(bf16[2,8,1536,768]{3,2,0,1:T(8,128)(2,1)} %maximum_bitcast_fusion), kind=kLoop, calls=%fused_computation.145 | loop fusion | bytes 75497472 | tf_op jit(solution)/shard_map/slice | solution.py:59
  542.1 575.5 %while.10 = (s32[]{:T(128)}, bf16[3,2,256,768]{3,2,1,0:T(8,128)(2,1)}, s32[3]{0:T(128)S(1)}, pred[6,27]{1,0:T(8,128)(4,1)S(1)}, bf16[6,256,768]{2,1,0:T(8,128)(2...) while((s32[]{:T(128)}, ...), condition=%wide.region_17.18_spmd, body=%wide.region_4.17_spmd.sunk | while | flops 11105987584 | bytes 443850720 | solution.py:100
  544.0 15.5 %gather_fusion.1 = bf16[54,256,768]{2,1,0:T(8,128)(2,1)} fusion(bf16[48,256,768]{2,1,0:T(8,128)(2,1)} %get-tuple-element.204, s32[1024]{0:T(1024)S(1)} %pad_clamp_fusion.3), kind=kCustom, calls=%fused_computation.clone.1 | custom fusion | bytes 42467544 | tf_op jit(solution)/shard_map/while/body/eval_jaxpr/gather | solution.py:71
  559.5 9.0 fusion.232
  568.7 10.7 fusion.233
  579.4 9.2 fusion.234
  588.6 9.0 fusion.235
  597.6 9.1 fusion.236
  606.8 31.3 %fusion.237 = (f32[2,256]{1,0:T(2,128)S(1)}, f32[2,256]{1,0:T(2,128)S(1)}, f32[2,256]{1,0:T(2,128)S(1)}, f32[2,256]{1,0:T(2,128)S(1)}, f32[2,256]{1,0:T(2,128)S(...) fusion(f32[2,256,6912]{2,1,0:T(8,128)} %get-tuple-element.151, f32[2,256]{1,0:T(2,128)S(1)} %get-tuple-element.152, ...), kind=kOutput, calls=%fused_computation.33.clone.1 | convolution fusion | flops 976745472 | bytes 88634888 | tf_op jit(solution)/shard_map/while/body/eval_jaxpr/tqd,tkd->tqk/dot_general | solution.py:79
  638.1 21.1 %fusion.239 = (f32[2,256]{1,0:T(2,128)S(1)}, f32[2,256]{1,0:T(2,128)S(1)}, f32[2,256]{1,0:T(2,128)S(1)}, f32[2,256]{1,0:T(2,128)S(1)}) fusion(f32[2,256,6912]{2,1,0:T(8,128)} %fusion.236, f32[2,256]{1,0:T(2,128)S(1)} %get-tuple-element.156, pred[2,6912]{1,0:T(4,128)(4,1)S(1)} %bitcast.63, f32[2,256]{1,0:T(2,128)S(1)} %get-tuple-element.155, ...), kind=kLoop, calls=%fused_computation.31.clone.1 | loop fusion | flops 56621056 | bytes 56653312 | tf_op jit(solution)/shard_map/while/body/eval_jaxpr/reduce_sum | solution.py:90
  659.2 15.6 %gather_fusion = bf16[54,256,768]{2,1,0:T(8,128)(2,1)} fusion(bf16[48,256,768]{2,1,0:T(8,128)(2,1)} %get-tuple-element.205, s32[1024]{0:T(1024)S(1)} %pad_clamp_fusion.3), kind=kCustom, calls=%fused_computation.1.clone.1 | custom fusion | bytes 42467544 | tf_op jit(solution)/shard_map/while/body/eval_jaxpr/gather | solution.py:72
  674.8 9.5 fusion.238
  684.4 9.5 fusion.240
  693.9 9.6 fusion.241
  703.5 9.8 fusion.242
  713.2 9.6 fusion.243
  722.8 9.6 fusion.244
  735.5 15.6 %gather_fusion.1 = bf16[54,256,768]{2,1,0:T(8,128)(2,1)} fusion(bf16[48,256,768]{2,1,0:T(8,128)(2,1)} %get-tuple-element.204, s32[1024]{0:T(1024)S(1)} %pad_clamp_fusion.3), kind=kCustom, calls=%fused_computation.clone.1 | custom fusion | bytes 42467544 | tf_op jit(solution)/shard_map/while/body/eval_jaxpr/gather | solution.py:71
  751.1 9.0 fusion.232
  760.3 10.7 fusion.233
  771.0 9.2 fusion.234
  780.2 9.0 fusion.235
  789.2 9.1 fusion.236
  798.3 31.1 %fusion.237 = (f32[2,256]{1,0:T(2,128)S(1)}, f32[2,256]{1,0:T(2,128)S(1)}, f32[2,256]{1,0:T(2,128)S(1)}, f32[2,256]{1,0:T(2,128)S(1)}, f32[2,256]{1,0:T(2,128)S(...) fusion(f32[2,256,6912]{2,1,0:T(8,128)} %get-tuple-element.151, f32[2,256]{1,0:T(2,128)S(1)} %get-tuple-element.152, ...), kind=kOutput, calls=%fused_computation.33.clone.1 | convolution fusion | flops 976745472 | bytes 88634888 | tf_op jit(solution)/shard_map/while/body/eval_jaxpr/tqd,tkd->tqk/dot_general | solution.py:79
  829.4 21.1 %fusion.239 = (f32[2,256]{1,0:T(2,128)S(1)}, f32[2,256]{1,0:T(2,128)S(1)}, f32[2,256]{1,0:T(2,128)S(1)}, f32[2,256]{1,0:T(2,128)S(1)}) fusion(f32[2,256,6912]{2,1,0:T(8,128)} %fusion.236, f32[2,256]{1,0:T(2,128)S(1)} %get-tuple-element.156, pred[2,6912]{1,0:T(4,128)(4,1)S(1)} %bitcast.63, f32[2,256]{1,0:T(2,128)S(1)} %get-tuple-element.155, ...), kind=kLoop, calls=%fused_computation.31.clone.1 | loop fusion | flops 56621056 | bytes 56653312 | tf_op jit(solution)/shard_map/while/body/eval_jaxpr/reduce_sum | solution.py:90
  850.5 15.8 %gather_fusion = bf16[54,256,768]{2,1,0:T(8,128)(2,1)} fusion(bf16[48,256,768]{2,1,0:T(8,128)(2,1)} %get-tuple-element.205, s32[1024]{0:T(1024)S(1)} %pad_clamp_fusion.3), kind=kCustom, calls=%fused_computation.1.clone.1 | custom fusion | bytes 42467544 | tf_op jit(solution)/shard_map/while/body/eval_jaxpr/gather | solution.py:72
  866.4 9.6 fusion.238
  875.9 9.6 fusion.240
  885.5 9.6 fusion.241
  895.0 9.9 fusion.242
  905.0 9.6 fusion.243
  914.6 9.6 fusion.244
  927.0 15.6 %gather_fusion.1 = bf16[54,256,768]{2,1,0:T(8,128)(2,1)} fusion(bf16[48,256,768]{2,1,0:T(8,128)(2,1)} %get-tuple-element.204, s32[1024]{0:T(1024)S(1)} %pad_clamp_fusion.3), kind=kCustom, calls=%fused_computation.clone.1 | custom fusion | bytes 42467544 | tf_op jit(solution)/shard_map/while/body/eval_jaxpr/gather | solution.py:71
  942.6 9.1 fusion.232
  951.8 10.7 fusion.233
  962.5 9.2 fusion.234
  971.7 9.0 fusion.235
  980.7 9.1 fusion.236
  989.9 31.1 %fusion.237 = (f32[2,256]{1,0:T(2,128)S(1)}, f32[2,256]{1,0:T(2,128)S(1)}, f32[2,256]{1,0:T(2,128)S(1)}, f32[2,256]{1,0:T(2,128)S(1)}, f32[2,256]{1,0:T(2,128)S(...) fusion(f32[2,256,6912]{2,1,0:T(8,128)} %get-tuple-element.151, f32[2,256]{1,0:T(2,128)S(1)} %get-tuple-element.152, ...), kind=kOutput, calls=%fused_computation.33.clone.1 | convolution fusion | flops 976745472 | bytes 88634888 | tf_op jit(solution)/shard_map/while/body/eval_jaxpr/tqd,tkd->tqk/dot_general | solution.py:79
  1021.0 21.1 %fusion.239 = (f32[2,256]{1,0:T(2,128)S(1)}, f32[2,256]{1,0:T(2,128)S(1)}, f32[2,256]{1,0:T(2,128)S(1)}, f32[2,256]{1,0:T(2,128)S(1)}) fusion(f32[2,256,6912]{2,1,0:T(8,128)} %fusion.236, f32[2,256]{1,0:T(2,128)S(1)} %get-tuple-element.156, pred[2,6912]{1,0:T(4,128)(4,1)S(1)} %bitcast.63, f32[2,256]{1,0:T(2,128)S(1)} %get-tuple-element.155, ...), kind=kLoop, calls=%fused_computation.31.clone.1 | loop fusion | flops 56621056 | bytes 56653312 | tf_op jit(solution)/shard_map/while/body/eval_jaxpr/reduce_sum | solution.py:90
  1042.1 16.0 %gather_fusion = bf16[54,256,768]{2,1,0:T(8,128)(2,1)} fusion(bf16[48,256,768]{2,1,0:T(8,128)(2,1)} %get-tuple-element.205, s32[1024]{0:T(1024)S(1)} %pad_clamp_fusion.3), kind=kCustom, calls=%fused_computation.1.clone.1 | custom fusion | bytes 42467544 | tf_op jit(solution)/shard_map/while/body/eval_jaxpr/gather | solution.py:72
  1058.1 9.5 fusion.238
  1067.6 9.5 fusion.240
  1077.2 9.6 fusion.241
  1086.8 9.7 fusion.242
  1096.5 9.6 fusion.243
  1106.0 9.6 fusion.244
  (70 shorter events, 32.8 us)
Async XLA Ops:
  0.0 296.7 %copy-start.3 = (s32[6,27]{1,0:T(8,128)S(1)}, s32[6,27]{1,0:T(8,128)}, u32[]{:S(2)}) copy-start(s32[6,27]{1,0:T(8,128)} %param.13) | copy-start | bytes 1948
  0.0 296.8 %copy-start.4 = (f32[768]{0:T(1024)S(1)}, f32[768]{0:T(1024)}, u32[]{:S(2)}) copy-start(f32[768]{0:T(1024)} %param.11) | copy-start | bytes 9220
  26.3 55.4 %collective-permute-start = (bf16[2,1536,768]{2,1,0:T(8,128)(2,1)S(1)}, bf16[2,1536,768]{2,1,0:T(8,128)(2,1)S(1)}, u32[]{:S(2)}, u32[]{:S(2)}) collective-permute-start(bf16[2,1536,768]{2,1,0:T(8,128)(2,1)S(1)} %pad_maximum_fusion), channel_id=1, source_target_pairs={{0,4},{4,8},{8,12},{12,16},{16,20},{20,24},{24,28},{28,0},{1,5},{5... | collective-permute-start | bytes 14155784 | tf_op jit(solution)/shard_map/ppermute | solution.py:26
  81.7 2.2 copy-start.1
  83.9 105.6 %collective-permute-start.1 = (bf16[2,1536,768]{2,1,0:T(8,128)(2,1)S(1)}, bf16[2,1536,768]{2,1,0:T(8,128)(2,1)S(1)}, u32[]{:S(2)}, u32[]{:S(2)}) collective-permute-start(bf16[2,1536,768]{2,1,0:T(8,128)(2,1)S(1)} %collective-permute-done), channel_id=1, source_target_pairs={{0,4},{4,8},{8,12},{12,16},{16,20},{20,24},{24,28},{28,0},{1,5},{5... | collective-permute-start | bytes 14155784 | tf_op jit(solution)/shard_map/ppermute | solution.py:26
  83.9 107.7 %collective-permute-start.4 = (bf16[2,1536,768]{2,1,0:T(8,128)(2,1)S(1)}, bf16[2,1536,768]{2,1,0:T(8,128)(2,1)}, u32[]{:S(2)}, u32[]{:S(2)}) collective-permute-start(bf16[2,1536,768]{2,1,0:T(8,128)(2,1)S(1)} %pad_maximum_fusion), channel_id=1, source_target_pairs={{4,0},{8,4},{12,8},{16,12},{20,16},{24,20},{28,24},{0,28},{5,1},{9... | collective-permute-start | bytes 14155784 | tf_op jit(solution)/shard_map/ppermute | solution.py:28
  189.5 2.1 copy-start.2
  191.6 105.1 %collective-permute-start.2 = (bf16[2,1536,768]{2,1,0:T(8,128)(2,1)S(1)}, bf16[2,1536,768]{2,1,0:T(8,128)(2,1)}, u32[]{:S(2)}, u32[]{:S(2)}) collective-permute-start(bf16[2,1536,768]{2,1,0:T(8,128)(2,1)S(1)} %collective-permute-done.1), channel_id=1, source_target_pairs={{0,4},{4,8},{8,12},{12,16},{16,20},{20,24},{24,28},{28,0},{1,5},{5... | collective-permute-start | bytes 14155784 | tf_op jit(solution)/shard_map/ppermute | solution.py:26
  191.6 109.0 %collective-permute-start.5 = (bf16[2,1536,768]{2,1,0:T(8,128)(2,1)}, bf16[2,1536,768]{2,1,0:T(8,128)(2,1)}, u32[]{:S(2)}, u32[]{:S(2)}) collective-permute-start(bf16[2,1536,768]{2,1,0:T(8,128)(2,1)} %collective-permute-done.4), channel_id=1, source_target_pairs={{4,0},{8,4},{12,8},{16,12},{20,16},{24,20},{28,24},{0,28},{5,1},{9... | collective-permute-start | bytes 14155784 | tf_op jit(solution)/shard_map/ppermute | solution.py:28
  296.7 106.0 %collective-permute-start.3 = (bf16[2,1536,768]{2,1,0:T(8,128)(2,1)}, bf16[2,1536,768]{2,1,0:T(8,128)(2,1)}, u32[]{:S(2)}, u32[]{:S(2)}) collective-permute-start(bf16[2,1536,768]{2,1,0:T(8,128)(2,1)} %collective-permute-done.2), channel_id=1, source_target_pairs={{0,4},{4,8},{8,12},{12,16},{16,20},{20,24},{24,28},{28,0},{1,5},{5... | collective-permute-start | bytes 14155784 | tf_op jit(solution)/shard_map/ppermute | solution.py:26
  296.7 115.9 %slice-start.2 = ((s8[4718592]{0:T(1024)(128)(4,1)}), s8[4194304]{0:T(1024)(128)(4,1)S(1)}, s32[]{:S(2)}) async-start(s8[4718592]{0:T(1024)(128)(4,1)} %bitcast.74), calls=%async_computation.2 | async-start | bytes 8388608
  300.6 112.0 %slice-start.3 = ((s8[4718592]{0:T(1024)(128)(4,1)}), s8[524288]{0:T(1024)(128)(4,1)S(1)}, s32[]{:S(2)}) async-start(s8[4718592]{0:T(1024)(128)(4,1)} %bitcast.74), calls=%async_computation.3 | async-start | bytes 1048576
  300.6 114.4 %slice-start = ((s8[4718592]{0:T(1024)(128)(4,1)}), s8[4194304]{0:T(1024)(128)(4,1)S(1)}, s32[]{:S(2)}) async-start(s8[4718592]{0:T(1024)(128)(4,1)} %bitcast.72), calls=%async_computation | async-start | bytes 8388608
  300.6 128.9 %collective-permute-start.6 = (bf16[2,1536,768]{2,1,0:T(8,128)(2,1)}, bf16[2,1536,768]{2,1,0:T(8,128)(2,1)S(1)}, u32[]{:S(2)}, u32[]{:S(2)}) collective-permute-start(bf16[2,1536,768]{2,1,0:T(8,128)(2,1)} %collective-permute-done.5), channel_id=1, source_target_pairs={{4,0},{8,4},{12,8},{16,12},{20,16},{24,20},{28,24},{0,28},{5,1},{9... | collective-permute-start | bytes 14155784 | tf_op jit(solution)/shard_map/ppermute | solution.py:28
  407.5 7.5 slice-start.1
  407.5 9.9 copy-start
